TPU v7x, 512 devices: a whole 4x4x16 slice. The times are simulated.
512 devices in a mesh: dp: 128 (over x, z, core), bin: 4 (over y).
Axes of the slice: x: 4, y: 4, z: 16, core: 2. Of those that a mesh axis runs over, the one named last changes fastest.
Arguments:
- features: bfloat16 [65536, 2, 2048], P(('dp', 'bin')), may hold values from -90 to 90
- head_weight: bfloat16 [2048, 1024], P('bin'), may hold values from -9 to 9
- bin_of_row: int32 [65536, 1], P(('dp', 'bin')), may hold values from 0 to 191; in each aligned block of 128 rows (0 to 127, 128 to 255, ...) at most 2 rows name the same one
- bin_owner: int32 [192], replicated, may hold values from 0 to 127, never falling along the last dimension, each value on 1 to 2 neighbouring positions
- bin_link: int32 [192], replicated, may hold values 0 or 1
Outputs:
- grad_rows: bfloat16 [65536, 2, 1024], P(('dp', 'bin'))
- grad_weight: float32 [2048, 1024], P(('bin', 'dp'))
Inputs may be any that keep to these rules, and one draw needn't show every extreme that they name: `bin_of_row`: in the rows of one device no bin appears more than 2 times. `bin_owner`: never falls; every owner holds 1 to 2 consecutive bins.
All inputs are finite; a program needn't handle non-finite values.
Results may differ from a plain program's by a relative error of at most 0.012.
Values may be sent and summed in bfloat16 or wider, within the bound.
No kernel may reach another device: no remote copies, remote signals or barrier semaphores. Data moves between devices by JAX's collectives and lax.ppermute only.
A program may use at most 64 MiB of HBM per device.

v0:
```python
import jax
import jax.numpy as jnp
from jax import lax
from jax.sharding import Mesh
from jax.sharding import PartitionSpec as P

MOSTB = 2
SOFTMAX_TEMP_SCALE = 0.1
DP_PARTS = (("dx", 4), ("dz", 16), ("dc", 2))
DP = tuple((name for name, _ in DP_PARTS))
EMPTY_MARK = 4.0


def allowed_mask(valid, first, bin_link, group_slots, per_bin):
    per_owner = per_bin * MOSTB
    position = jnp.arange(group_slots, dtype=jnp.int32)
    local_bin = position % per_owner // per_bin
    padded = jnp.concatenate([bin_link, jnp.zeros((MOSTB,), jnp.int32)])
    nearby = lax.dynamic_slice(padded, (first,), (MOSTB,))
    lower = jnp.minimum(local_bin[:, None], local_bin[None, :])
    linked = jnp.zeros((group_slots, group_slots), jnp.int32)
    for height in range(MOSTB):
        linked = linked + jnp.where(lower == height, nearby[height], 0)
    spacing = jnp.abs(local_bin[:, None] - local_bin[None, :])
    paired = valid[:, None] & valid[None, :]
    allowed = paired & ((spacing == 0) | (spacing == 1) & (linked == 1))
    allowed = allowed | (position[:, None] == position[None, :])
    return allowed.astype(jnp.float32)


def contrast(query_rows, key_matrix, allowed, valid):
    similarity_scores = (
        lax.dot_general(
            query_rows, key_matrix, (((1,), (1,)), ((), ())), preferred_element_type=jnp.float32
        )
        / SOFTMAX_TEMP_SCALE
    )
    weights = allowed * jnp.exp(similarity_scores)
    shares = weights / jnp.sum(weights, axis=1, keepdims=True)
    position = jnp.arange(query_rows.shape[0], dtype=jnp.int32)
    diagonal = (position[:, None] == position[None, :]).astype(jnp.float32)
    logit_gradient = ((shares - diagonal) * valid[:, None]).astype(jnp.bfloat16)
    query_gradient = (
        jnp.dot(logit_gradient, key_matrix, preferred_element_type=jnp.float32) / SOFTMAX_TEMP_SCALE
    ).astype(jnp.bfloat16)
    key_gradient_rows = (
        lax.dot_general(
            logit_gradient, query_rows, (((0,), (0,)), ((), ())), preferred_element_type=jnp.float32
        )
        / SOFTMAX_TEMP_SCALE
    ).astype(jnp.bfloat16)
    return jnp.stack([query_gradient, key_gradient_rows], axis=1)


def dp_index():
    index = 0
    for name, size in DP_PARTS:
        index = index * size + lax.axis_index(name)
    return index


def local(features, head_weight, bin_of_row, bin_owner, bin_link):
    rows_dev, views, feat_dim = features.shape
    part_rows, emb_dim = head_weight.shape
    sources = 1
    for _, size in DP_PARTS:
        sources *= size
    bins_n = lax.axis_size("bin")
    bin_count = bin_owner.shape[0]
    per_bin = max(2, 2 * rows_dev // bin_count)
    per_owner = per_bin * MOSTB
    group_slots = sources * per_owner
    flat = features.reshape(rows_dev * views, feat_dim)
    folded = jnp.dot(
        flat,
        lax.all_gather(head_weight, "bin", axis=0, tiled=True),
        preferred_element_type=jnp.float32,
    )
    embedded = folded.reshape(rows_dev, views, emb_dim)
    scale = lax.rsqrt(jnp.sum(embedded * embedded, axis=2, keepdims=True) + 1e-06)
    unit = embedded * scale
    sent = unit.astype(jnp.bfloat16)
    row_bins = bin_of_row[:, 0]
    lookup = row_bins[:, None] == jnp.arange(bin_count, dtype=jnp.int32)[None, :]
    owner = jnp.sum(jnp.where(lookup, bin_owner[None, :], 0), axis=1)
    first_by_bin = jnp.sum((bin_owner[None, :] < bin_owner[:, None]).astype(jnp.int32), axis=1)
    local_bin = row_bins - jnp.sum(jnp.where(lookup, first_by_bin[None, :], 0), axis=1)
    order = jnp.arange(rows_dev, dtype=jnp.int32)
    earlier = (row_bins[:, None] == row_bins[None, :]) & (order[None, :] < order[:, None])
    seat = jnp.sum(earlier.astype(jnp.int32), axis=1)
    target = owner * per_owner + local_bin * per_bin + seat
    empty = jnp.zeros((group_slots, views, emb_dim), jnp.bfloat16).at[:, 0, 0].set(EMPTY_MARK)
    outbox = empty.at[target].set(sent)
    inbox = lax.all_to_all(
        outbox.reshape(sources, per_owner, views, emb_dim),
        DP,
        split_axis=0,
        concat_axis=0,
        tiled=True,
    )
    inbox = inbox.reshape(group_slots, views, emb_dim)
    valid = inbox[:, 0, 0] < 2.0
    inbox = jnp.where(valid[:, None, None], inbox, jnp.zeros_like(inbox))
    first = jnp.sum((bin_owner < dp_index()).astype(jnp.int32))
    allowed = allowed_mask(valid, first, bin_link, group_slots, per_bin)
    grads = contrast(inbox[:, 0], inbox[:, 1], allowed, valid.astype(jnp.float32))
    returned = lax.all_to_all(
        grads.reshape(sources, per_owner, views, emb_dim),
        DP,
        split_axis=0,
        concat_axis=0,
        tiled=True,
    )
    row_grads = returned.reshape(group_slots, views, emb_dim)[target].astype(jnp.float32)
    grad_rows = (
        scale * (row_grads - unit * jnp.sum(unit * row_grads, axis=2, keepdims=True))
    ).astype(jnp.bfloat16)
    columns = lax.all_to_all(
        features.reshape(rows_dev, views, bins_n, part_rows),
        "bin",
        split_axis=2,
        concat_axis=0,
        tiled=True,
    )
    outgrad = lax.all_gather(grad_rows, "bin", axis=0, tiled=True)
    count = columns.shape[0]
    sizes = [size for _, size in DP_PARTS]
    columns = columns.reshape(count * views, *sizes, part_rows // sources)
    columns = jnp.transpose(columns, (0, 3, 2, 1, 4)).reshape(count * views, part_rows)
    local_grad = lax.dot_general(
        columns,
        outgrad.reshape(count * views, emb_dim),
        (((0,), (0,)), ((), ())),
        preferred_element_type=jnp.float32,
    )
    for name in ("dc", "dz", "dx"):
        local_grad = lax.psum_scatter(local_grad, name, scatter_dimension=0, tiled=True)
    grad_weight = local_grad / rows_dev
    return (grad_rows, grad_weight)


def solution(mesh):
    sizes = [size for _, size in DP_PARTS]
    devices = mesh.devices.reshape(*sizes, mesh.devices.shape[1])
    parted = Mesh(devices, (*DP, "bin"))
    return jax.shard_map(
        local,
        mesh=parted,
        in_specs=(P((*DP, "bin"), None, None), P("bin", None), P((*DP, "bin"), None), P(), P()),
        out_specs=(P((*DP, "bin"), None, None), P(("bin", *DP), None)),
        check_vma=False,
    )
```

profile of v0, /device:TPU:8, one launch (start us, length us, event | category | flops | bytes accessed | tf_op | source)
XLA Modules:
  0.0 661.2 jit_solution(16799873341460603890)
XLA Ops:
  7.2 0.7 all-gather.3.cloned.1.call-update
  7.9 0.9 convert_reduce_fusion.1
  8.8 0.9 convert_reduce_fusion
  9.8 0.8 select_reduce_fusion.1
  10.6 0.7 fusion.28
  11.2 58.6 %all-gather.3.cloned.1.call-done = bf16[2048,1024]{1,0:T(8,128)(2,1)} async-done(((bf16[512,1024]{1,0:T(8,128)(2,1)}), bf16[2048,1024]{1,0:T(8,128)(2,1)}) %all-gather.3.cloned.1.call-update) | async-done | bytes 4194320 | tf_op jit(solution)/shard_map/all_gather | solution.py:76
  69.8 3.9 multiply_reduce_fusion
  73.8 0.1 multiply_convert_fusion.3
  73.9 0.8 copy-done.3
  74.7 0.5 copy.33
  75.3 1.1 scatter.12
  76.4 4.3 scatter_fusion
  80.7 1.3 copy-done
  82.0 17.0 %all-to-all-start = ((bf16[128,4,2,1024]{3,2,1,0:T(2,128)(2,1)}), bf16[128,4,2,1024]{3,2,1,0:T(2,128)(2,1)S(1)}, u32[]{:S(2)}, u32[]{:S(2)}) async-start(bf16[128,4,2,1024]{3,2,1,0:T(2,128)(2,1)} %bitcast.64), calls=%async_computation | async-start | bytes 4194304 | tf_op jit(solution)/shard_map/all_to_all | solution.py:94
  99.0 0.6 fusion.27
  101.7 0.6 fusion.31
  102.3 95.6 %all-to-all-done = bf16[128,4,2,1024]{3,2,1,0:T(2,128)(2,1)S(1)} async-done(((bf16[128,4,2,1024]{3,2,1,0:T(2,128)(2,1)}), bf16[128,4,2,1024]{3,2,1,0:T(2,128)(2,1)S(1)}, u32[]{:S(2)}, u32[]{:S(2)}) %all-to-all-start) | async-done | bytes 2097184 | tf_op jit(solution)/shard_map/all_to_all | solution.py:94
  197.8 0.6 copy.44
  198.4 0.2 compare_reduce_fusion
  198.6 0.4 broadcast_select_fusion
  199.0 2.7 fusion.32
  201.7 0.8 multiply_convert_fusion.1
  202.5 0.7 multiply_convert_fusion
  203.2 0.4 stack.9
  203.6 0.4 stack.10
  204.0 2.7 pad_maximum_fusion
  206.8 9.2 %all-to-all-start.1 = ((bf16[128,4,2,1024]{3,1,2,0:T(4,128)(2,1)}), bf16[128,4,2,1024]{3,1,2,0:T(4,128)(2,1)S(1)}, u32[]{:S(2)}, u32[]{:S(2)}) async-start(bf16[128,4,2,1024]{3,1,2,0:T(4,128)(2,1)} %pad_maximum_fusion), calls=%async_computation.1 | async-start | bytes 4194304 | tf_op jit(solution)/shard_map/all_to_all | solution.py:107
  216.0 98.8 %all-to-all-done.1 = bf16[128,4,2,1024]{3,1,2,0:T(4,128)(2,1)S(1)} async-done(((bf16[128,4,2,1024]{3,1,2,0:T(4,128)(2,1)}), bf16[128,4,2,1024]{3,1,2,0:T(4,128)(2,1)S(1)}, u32[]{:S(2)}, u32[]{:S(2)}) %all-to-all-start.1) | async-done | bytes 2097184 | tf_op jit(solution)/shard_map/all_to_all | solution.py:107
  314.8 3.8 copy.37
  318.6 3.3 gather_fusion
  321.9 2.1 fusion.9
  324.1 0.7 copy.61
  324.8 23.8 %all_to_all.25 = bf16[128,2,4,512]{3,1,0,2:T(2,128)(2,1)S(1)} all-to-all(bf16[128,2,4,512]{3,1,0,2:T(2,128)(2,1)S(1)} %bitcast.66), channel_id=1, replica_groups=mesh['dx'=4,'dz'=16,'dc'=2,'bin'=4] {'bin'}, dimensions={2} | all-to-all | bytes 2097152 | tf_op jit(solution)/shard_map/all_to_all | solution.py:118
  348.6 73.1 %reshape.155 = bf16[1024,4,16,2,4]{4,3,2,1,0:T(2,128)(2,1)} reshape(bf16[4,128,2,1,512]{4,2,1,0,3:T(2,128)(2,1)S(1)} %bitcast.65) | data formatting | bytes 2097152 | tf_op jit(solution)/shard_map/reshape | solution.py:128
  421.7 76.1 %copy.41 = bf16[1024,2,16,4,4]{0,4,3,2,1:T(4,128)(2,1)S(1)} copy(bf16[1024,2,16,4,4]{4,1,2,3,0:T(2,128)(2,1)} %bitcast.61) | data formatting | bytes 2097152 | tf_op jit(solution)/shard_map/transpose | solution.py:129
  497.8 0.3 reshape.156
  498.1 3.7 copy.39
  501.9 2.2 reshape.153
  504.1 4.2 convolution_bitcast_fusion
  508.5 11.2 %reduce-scatter.6.cloned.1.call-done = f32[256,1024]{0,1:T(8,128)} async-done(((f32[512,1024]{0,1:T(8,128)}), f32[256,1024]{0,1:T(8,128)}) %reduce-scatter.6.cloned.1.call-update) | async-done | bytes 1048592 | tf_op jit(solution)/shard_map/reduce_scatter | solution.py:137
  519.6 2.5 copy.45
  522.3 72.0 %reduce-scatter.8.cloned.1.call-done = f32[16,1024]{1,0:T(8,128)} async-done(((f32[256,1024]{1,0:T(8,128)}), f32[16,1024]{1,0:T(8,128)}) %reduce-scatter.8.cloned.1.call-update) | async-done | bytes 65552
  594.3 1.8 copy.46
  596.2 1.3 dynamic-slice.6
  598.1 1.3 copy.42
  599.4 53.2 %all-reduce.4.cloned.1.call-done = f32[16,1024]{0,1:T(8,128)} async-done(((f32[16,1024]{0,1:T(8,128)}), f32[16,1024]{0,1:T(8,128)}) %all-reduce.4.cloned.1.call-update) | async-done | bytes 65552
  652.7 1.2 dynamic-slice_multiply_fusion
  653.9 0.8 copy.43
  (29 shorter events, 0.4 us)
Async XLA Ops:
  7.2 62.7 %all-gather.3.cloned.1.call-start = ((), (), s32[]{:S(2)}) async-start(), calls=%async_computation.5 | async-start | bytes 5242880 | tf_op jit(solution)/shard_map/all_gather | solution.py:76
  73.7 1.0 copy-start.3
  73.7 1.5 copy-start.6
  80.7 1.4 copy-start
  82.0 17.0 %copy-start.5 = (s32[192]{0:T(256)S(1)}, s32[192]{0:T(256)}, u32[]{:S(2)}) copy-start(s32[192]{0:T(256)} %param.10) | copy-start | bytes 2308
  82.0 19.6 %copy-start.7 = (s32[192]{0:T(256)S(1)}, s32[192]{0:T(256)}, u32[]{:S(2)}) copy-start(s32[192]{0:T(256)} %param.11) | copy-start | bytes 2308
  82.0 115.8 %all-to-all-start = ((bf16[128,4,2,1024]{3,2,1,0:T(2,128)(2,1)}), bf16[128,4,2,1024]{3,2,1,0:T(2,128)(2,1)S(1)}, u32[]{:S(2)}, u32[]{:S(2)}) async-start(bf16[128,4,2,1024]{3,2,1,0:T(2,128)(2,1)} %bitcast.64), calls=%async_computation | async-start | bytes 4194304 | tf_op jit(solution)/shard_map/all_to_all | solution.py:94
  206.8 108.0 %all-to-all-start.1 = ((bf16[128,4,2,1024]{3,1,2,0:T(4,128)(2,1)}), bf16[128,4,2,1024]{3,1,2,0:T(4,128)(2,1)S(1)}, u32[]{:S(2)}, u32[]{:S(2)}) async-start(bf16[128,4,2,1024]{3,1,2,0:T(4,128)(2,1)} %pad_maximum_fusion), calls=%async_computation.1 | async-start | bytes 4194304 | tf_op jit(solution)/shard_map/all_to_all | solution.py:107
  216.0 282.2 %all-gather.5.cloned.1.call-start = ((), (), s32[]{:S(2)}) async-start(), calls=%async_computation.6 | async-start | bytes 2621440 | tf_op jit(solution)/shard_map/all_gather | solution.py:125
  216.0 105.8 %copy-start.4 = (f32[128,2,1024]{2,0,1:T(8,128)S(1)}, f32[128,2,1024]{2,0,1:T(8,128)}, u32[]{:S(2)}) copy-start(f32[128,2,1024]{2,0,1:T(8,128)} %copy-done.3) | copy-start | bytes 3145732
  318.6 5.5 copy-start.2
  324.0 195.6 %reduce-scatter.6.cloned.1.call-start = ((), (), s32[]{:S(2)}) async-start(), calls=%async_computation.7 | async-start | bytes 3145728 | tf_op jit(solution)/shard_map/reduce_scatter | solution.py:137
  508.4 89.7 %copy-start.1 = (bf16[128,2,1024]{2,0,1:T(8,128)(2,1)S(1)}, bf16[128,2,1024]{2,0,1:T(8,128)(2,1)}, u32[]{:S(2)}) copy-start(bf16[128,2,1024]{2,0,1:T(8,128)(2,1)} %fusion.9) | copy-start | bytes 1572868
  508.4 85.9 %reduce-scatter.8.cloned.1.call-start = ((), (), s32[]{:S(2)}) async-start(), calls=%async_computation.8 | async-start | bytes 1114112
  522.2 130.5 %all-reduce.4.cloned.1.call-start = ((), (), s32[]{:S(2)}) async-start(), calls=%async_computation.9 | async-start | bytes 1048576
Sparse Core Ops, SparseCore 0:
  10.1 59.6 all-gather.2
  324.1 35.2 all-gather.4
  508.5 11.0 reduce-scatter.5
  522.5 71.7 reduce-scatter.7
  596.5 56.1 all-reduce.3
where the time goes:
time: 663 us; the launch traced here: 661 us
  waiting for transfers between devices  390 us (59%)
  local copies, waits for them, and re-layouts  181 us (27%)
  starting transfers between devices  26.4 us (4%)
  blocking collectives  23.8 us (4%)
  between operations  16.6 us (3%)
  matrix products  12.3 us (2%)
  other arithmetic  10.7 us (2%)
    unnamed x7, waiting for transfers between devices  126 us
    all_to_all x1, waiting for transfers between devices, local(): lax.all_to_all(grads.reshape(sources, per_owner, views, emb_dim), DP, spl...  98.8 us
    all_to_all x1, waiting for transfers between devices, local(): lax.all_to_all(outbox.reshape(sources, per_owner, views, emb_dim), DP, sp...  95.6 us
    transpose x1, local copies, waits for them, and re-layouts, local(): jnp.transpose(columns, (0, 3, 2, 1, 4)).reshape(count * views, part_rows)  76.1 us
    reshape x1, local copies, waits for them, and re-layouts, local(): columns = columns.reshape(count * views, *sizes, part_rows // sources)  73.1 us
    all_gather x1, waiting for transfers between devices, local(): lax.all_gather(head_weight, 'bin', axis=0, tiled=True)  58.6 us
    all_to_all x1, blocking collectives, local(): lax.all_to_all(features.reshape(rows_dev, views, bins_n, part_rows), 'bin...  23.8 us
    all_to_all x1, starting transfers between devices, local(): lax.all_to_all(outbox.reshape(sources, per_owner, views, emb_dim), DP, sp...  17 us
  transfers between devices with their start and end apart: 7, of which 6 were waited for; matrix products, arithmetic and copies ran while one was open for 24% of the time, Pallas kernels for 0%

commit v1 on v0

--- a/solution.py
+++ b/solution.py
@@ -73,7 +73,9 @@
     flat = features.reshape(rows_dev * views, feat_dim)
     folded = jnp.dot(
         flat,
-        lax.all_gather(head_weight, "bin", axis=0, tiled=True),
+        jnp.concatenate(
+            lax.all_to_all(jnp.stack([head_weight] * lax.axis_size("bin")), "bin", 0, 0), axis=0
+        ),
         preferred_element_type=jnp.float32,
     )
     embedded = folded.reshape(rows_dev, views, emb_dim)

time: 663 us -> 660 us (level)
  waiting for transfers between devices: 390 us -> 373 us
  starting transfers between devices: 26.4 us -> 40.1 us
    all_gather x1 -> x0, waiting for transfers between devices: 58.6 us -> none  [local(): lax.all_gather(head_weight, 'bin', axis=0, tiled=True)]
    all_to_all x0 -> x1, waiting for transfers between devices: none -> 41.9 us  [local(): lax.all_to_all(jnp.stack([head_weight] * lax.axis_size('bin')), 'bin', 0, 0)]
    all_to_all x0 -> x1, starting transfers between devices: none -> 10.8 us  [local(): lax.all_to_all(jnp.stack([head_weight] * lax.axis_size('bin')), 'bin', 0, 0)]
    unnamed x7 -> x6, waiting for transfers between devices: 126 us -> 125 us
  transfers between devices with their start and end apart: 7 -> 7, of which waited for: 6 -> 6; matrix products, arithmetic and copies ran while one was open for 24% -> 23% of each run, Pallas kernels for 0% -> 0%
where the time goes in v1:
time: 660 us; the launch traced here: 658 us
  waiting for transfers between devices  373 us (57%)
  local copies, waits for them, and re-layouts  185 us (28%)
  starting transfers between devices  40.1 us (6%)
  blocking collectives  23.7 us (4%)
  between operations  16.6 us (3%)
  matrix products  11.9 us (2%)
  other arithmetic  7.9 us (1%)
    unnamed x6, waiting for transfers between devices  125 us
    all_to_all x1, waiting for transfers between devices, local(): lax.all_to_all(grads.reshape(sources, per_owner, views, emb_dim), DP, spl...  98.8 us
    all_to_all x1, waiting for transfers between devices, local(): lax.all_to_all(outbox.reshape(sources, per_owner, views, emb_dim), DP, sp...  95.6 us
    transpose x1, local copies, waits for them, and re-layouts, local(): jnp.transpose(columns, (0, 3, 2, 1, 4)).reshape(count * views, part_rows)  76.1 us
    reshape x1, local copies, waits for them, and re-layouts, local(): columns = columns.reshape(count * views, *sizes, part_rows // sources)  73.1 us
    all_to_all x1, waiting for transfers between devices, local(): lax.all_to_all(jnp.stack([head_weight] * lax.axis_size('bin')), 'bin', 0, 0)  41.9 us
    all_to_all x1, blocking collectives, local(): lax.all_to_all(features.reshape(rows_dev, views, bins_n, part_rows), 'bin...  23.7 us
    all_to_all x1, starting transfers between devices, local(): lax.all_to_all(outbox.reshape(sources, per_owner, views, emb_dim), DP, sp...  19.9 us
  transfers between devices with their start and end apart: 7, of which 6 were waited for; matrix products, arithmetic and copies ran while one was open for 23% of the time, Pallas kernels for 0%

profile of v1, /device:TPU:8, one launch (start us, length us, event | category | flops | bytes accessed | tf_op | source)
XLA Modules:
  0.0 658.2 jit_solution(6494661817010972537)
XLA Ops:
  7.2 3.7 stack.16
  10.9 10.8 %all-to-all-start = ((bf16[4,512,1024]{2,1,0:T(8,128)(2,1)}), bf16[4,512,1024]{2,1,0:T(8,128)(2,1)}, u32[]{:S(2)}, u32[]{:S(2)}) async-start(bf16[4,512,1024]{2,1,0:T(8,128)(2,1)} %stack.16), calls=%async_computation | async-start | bytes 8388608 | tf_op jit(solution)/shard_map/all_to_all | solution.py:77
  21.7 0.2 convert_reduce_fusion.1
  21.9 0.2 convert_reduce_fusion
  22.1 0.1 select_reduce_fusion.1
  22.2 41.9 %all-to-all-done = bf16[4,512,1024]{2,1,0:T(8,128)(2,1)} async-done(((bf16[4,512,1024]{2,1,0:T(8,128)(2,1)}), bf16[4,512,1024]{2,1,0:T(8,128)(2,1)}, u32[]{:S(2)}, u32[]{:S(2)}) %all-to-all-start) | async-done | bytes 4194336 | tf_op jit(solution)/shard_map/all_to_all | solution.py:77
  64.1 3.6 multiply_reduce_fusion
  67.7 0.1 multiply_convert_fusion.3
  67.8 0.8 copy-done.4
  68.7 0.5 copy.33
  69.2 1.1 scatter.12
  70.3 4.3 scatter_fusion
  74.6 1.3 copy-done
  76.0 19.9 %all-to-all-start.1 = ((bf16[128,4,2,1024]{3,2,1,0:T(2,128)(2,1)}), bf16[128,4,2,1024]{3,2,1,0:T(2,128)(2,1)S(1)}, u32[]{:S(2)}, u32[]{:S(2)}) async-start(bf16[128,4,2,1024]{3,2,1,0:T(2,128)(2,1)} %bitcast.63), calls=%async_computation.1 | async-start | bytes 4194304 | tf_op jit(solution)/shard_map/all_to_all | solution.py:96
  95.9 0.6 fusion.26
  98.6 0.6 fusion.30
  99.1 95.6 %all-to-all-done.1 = bf16[128,4,2,1024]{3,2,1,0:T(2,128)(2,1)S(1)} async-done(((bf16[128,4,2,1024]{3,2,1,0:T(2,128)(2,1)}), bf16[128,4,2,1024]{3,2,1,0:T(2,128)(2,1)S(1)}, u32[]{:S(2)}, u32[]{:S(2)}) %all-to-all-start.1) | async-done | bytes 2097184 | tf_op jit(solution)/shard_map/all_to_all | solution.py:96
  194.7 0.6 copy.44
  195.3 0.2 compare_reduce_fusion
  195.5 0.4 broadcast_select_fusion
  195.9 2.7 fusion.31
  198.6 0.8 multiply_convert_fusion.1
  199.4 0.7 multiply_convert_fusion
  200.1 0.4 stack.17
  200.5 0.4 stack.18
  200.9 2.7 pad_maximum_fusion
  203.7 9.2 %all-to-all-start.2 = ((bf16[128,4,2,1024]{3,1,2,0:T(4,128)(2,1)}), bf16[128,4,2,1024]{3,1,2,0:T(4,128)(2,1)S(1)}, u32[]{:S(2)}, u32[]{:S(2)}) async-start(bf16[128,4,2,1024]{3,1,2,0:T(4,128)(2,1)} %pad_maximum_fusion), calls=%async_computation.2 | async-start | bytes 4194304 | tf_op jit(solution)/shard_map/all_to_all | solution.py:109
  212.9 98.8 %all-to-all-done.2 = bf16[128,4,2,1024]{3,1,2,0:T(4,128)(2,1)S(1)} async-done(((bf16[128,4,2,1024]{3,1,2,0:T(4,128)(2,1)}), bf16[128,4,2,1024]{3,1,2,0:T(4,128)(2,1)S(1)}, u32[]{:S(2)}, u32[]{:S(2)}) %all-to-all-start.2) | async-done | bytes 2097184 | tf_op jit(solution)/shard_map/all_to_all | solution.py:109
  311.7 3.8 copy.37
  315.5 3.3 gather_fusion
  318.8 2.1 fusion.7
  321.0 0.7 copy.61
  321.7 23.7 %all_to_all.30 = bf16[128,2,4,512]{3,1,0,2:T(2,128)(2,1)S(1)} all-to-all(bf16[128,2,4,512]{3,1,0,2:T(2,128)(2,1)S(1)} %bitcast.65), channel_id=1, replica_groups=mesh['dx'=4,'dz'=16,'dc'=2,'bin'=4] {'bin'}, dimensions={2} | all-to-all | bytes 2097152 | tf_op jit(solution)/shard_map/all_to_all | solution.py:120
  345.4 73.1 %reshape.161 = bf16[1024,4,16,2,4]{4,3,2,1,0:T(2,128)(2,1)} reshape(bf16[4,128,2,1,512]{4,2,1,0,3:T(2,128)(2,1)S(1)} %bitcast.64) | data formatting | bytes 2097152 | tf_op jit(solution)/shard_map/reshape | solution.py:130
  418.5 76.1 %copy.41 = bf16[1024,2,16,4,4]{0,4,3,2,1:T(4,128)(2,1)S(1)} copy(bf16[1024,2,16,4,4]{4,1,2,3,0:T(2,128)(2,1)} %bitcast.60) | data formatting | bytes 2097152 | tf_op jit(solution)/shard_map/transpose | solution.py:131
  494.6 0.3 reshape.162
  494.9 3.7 copy.39
  498.7 2.2 reshape.159
  500.9 4.2 convolution_bitcast_fusion
  505.3 11.2 %reduce-scatter.6.cloned.1.call-done = f32[256,1024]{0,1:T(8,128)} async-done(((f32[512,1024]{0,1:T(8,128)}), f32[256,1024]{0,1:T(8,128)}) %reduce-scatter.6.cloned.1.call-update) | async-done | bytes 1048592 | tf_op jit(solution)/shard_map/reduce_scatter | solution.py:139
  516.5 2.5 copy.45
  519.1 72.2 %reduce-scatter.8.cloned.1.call-done = f32[16,1024]{1,0:T(8,128)} async-done(((f32[256,1024]{1,0:T(8,128)}), f32[16,1024]{1,0:T(8,128)}) %reduce-scatter.8.cloned.1.call-update) | async-done | bytes 65552
  591.3 1.8 copy.46
  593.2 1.3 dynamic-slice.6
  595.1 1.3 copy.42
  596.4 53.2 %all-reduce.4.cloned.1.call-done = f32[16,1024]{0,1:T(8,128)} async-done(((f32[16,1024]{0,1:T(8,128)}), f32[16,1024]{0,1:T(8,128)}) %all-reduce.4.cloned.1.call-update) | async-done | bytes 65552
  649.6 1.2 dynamic-slice_multiply_fusion
  650.9 0.8 copy.43
  (33 shorter events, 0.4 us)
Async XLA Ops:
  10.9 10.8 %copy-start.8 = (s32[128,1]{0,1:T(1,128)S(1)}, s32[128,1]{0,1:T(1,128)}, u32[]{:S(2)}) copy-start(s32[128,1]{0,1:T(1,128)} %param.9) | copy-start | bytes 1540
  10.9 11.0 %copy-start.6 = (s32[192]{0:T(256)S(1)}, s32[192]{0:T(256)}, u32[]{:S(2)}) copy-start(s32[192]{0:T(256)} %param.10) | copy-start | bytes 2308
  10.9 53.2 %copy-start.2 = (bf16[128,2,2048]{2,1,0:T(2,128)(2,1)S(1)}, bf16[128,2,2048]{2,1,0:T(2,128)(2,1)}, u32[]{:S(2)}) copy-start(bf16[128,2,2048]{2,1,0:T(2,128)(2,1)} %param.7) | copy-start | bytes 3145732
  10.9 53.2 %all-to-all-start = ((bf16[4,512,1024]{2,1,0:T(8,128)(2,1)}), bf16[4,512,1024]{2,1,0:T(8,128)(2,1)}, u32[]{:S(2)}, u32[]{:S(2)}) async-start(bf16[4,512,1024]{2,1,0:T(8,128)(2,1)} %stack.16), calls=%async_computation | async-start | bytes 8388608 | tf_op jit(solution)/shard_map/all_to_all | solution.py:77
  67.7 1.0 copy-start.4
  67.7 1.5 copy-start.7
  74.6 1.4 copy-start
  76.0 22.5 %copy-start.9 = (s32[192]{0:T(256)S(1)}, s32[192]{0:T(256)}, u32[]{:S(2)}) copy-start(s32[192]{0:T(256)} %param.11) | copy-start | bytes 2308
  76.0 118.8 %all-to-all-start.1 = ((bf16[128,4,2,1024]{3,2,1,0:T(2,128)(2,1)}), bf16[128,4,2,1024]{3,2,1,0:T(2,128)(2,1)S(1)}, u32[]{:S(2)}, u32[]{:S(2)}) async-start(bf16[128,4,2,1024]{3,2,1,0:T(2,128)(2,1)} %bitcast.63), calls=%async_computation.1 | async-start | bytes 4194304 | tf_op jit(solution)/shard_map/all_to_all | solution.py:96
  203.7 108.0 %all-to-all-start.2 = ((bf16[128,4,2,1024]{3,1,2,0:T(4,128)(2,1)}), bf16[128,4,2,1024]{3,1,2,0:T(4,128)(2,1)S(1)}, u32[]{:S(2)}, u32[]{:S(2)}) async-start(bf16[128,4,2,1024]{3,1,2,0:T(4,128)(2,1)} %pad_maximum_fusion), calls=%async_computation.2 | async-start | bytes 4194304 | tf_op jit(solution)/shard_map/all_to_all | solution.py:109
  212.9 282.1 %all-gather.2.cloned.1.call-start = ((), (), s32[]{:S(2)}) async-start(), calls=%async_computation.6 | async-start | bytes 2621440 | tf_op jit(solution)/shard_map/all_gather | solution.py:127
  212.9 105.8 %copy-start.5 = (f32[128,2,1024]{2,0,1:T(8,128)S(1)}, f32[128,2,1024]{2,0,1:T(8,128)}, u32[]{:S(2)}) copy-start(f32[128,2,1024]{2,0,1:T(8,128)} %copy-done.4) | copy-start | bytes 3145732
  315.5 5.5 copy-start.3
  320.9 195.6 %reduce-scatter.6.cloned.1.call-start = ((), (), s32[]{:S(2)}) async-start(), calls=%async_computation.7 | async-start | bytes 3145728 | tf_op jit(solution)/shard_map/reduce_scatter | solution.py:139
  505.2 89.9 %copy-start.1 = (bf16[128,2,1024]{2,0,1:T(8,128)(2,1)S(1)}, bf16[128,2,1024]{2,0,1:T(8,128)(2,1)}, u32[]{:S(2)}) copy-start(bf16[128,2,1024]{2,0,1:T(8,128)(2,1)} %fusion.7) | copy-start | bytes 1572868
  505.2 86.1 %reduce-scatter.8.cloned.1.call-start = ((), (), s32[]{:S(2)}) async-start(), calls=%async_computation.8 | async-start | bytes 1114112
  519.0 130.6 %all-reduce.4.cloned.1.call-start = ((), (), s32[]{:S(2)}) async-start(), calls=%async_computation.9 | async-start | bytes 1048576
Sparse Core Ops, SparseCore 0:
  321.0 35.0 all-gather.1
  505.3 11.0 reduce-scatter.5
  519.5 71.7 reduce-scatter.7
  593.5 56.1 all-reduce.3
